TPU v7x, 512 devices: a whole 4x4x16 slice. The times are simulated.
512 devices in a mesh: path: 32 (over x, y, core), tensor: 16 (over z).
Axes of the slice: x: 4, y: 4, z: 16, core: 2. Of those that a mesh axis runs over, the one named last changes fastest.
Arguments:
- hidden_in: bfloat16 [12288, 2048], P(('path', 'tensor')), may hold values from -120 to 120
- teacher: bfloat16 [12288, 2048], P('path'), may hold values from -3 to 3
- params: bfloat16 [3, 3, 7168, 2048], P(None, None, ('tensor', 'path')), may hold values from -4 to 4
- momentum: float32 [3, 3, 7168, 2048], P(None, None, ('tensor', 'path')), may hold values from -3 to 3
- path_alive: int32 [32], replicated, may hold values from 0 to 1, as said below
- path_module: int32 [32], replicated, may hold values from 0 to 2, as said below
Outputs:
- new_params: bfloat16 [3, 3, 7168, 2048], P(None, None, ('tensor', 'path'))
- new_momentum: float32 [3, 3, 7168, 2048], P(None, None, ('tensor', 'path'))
Inputs may be any that keep to these rules, and one draw needn't show every extreme that they name: `path_alive`: at least one path is dead. `path_module`: every one of the 3 modules is used by at least one path whose path_alive entry is 1.
All inputs are finite; a program needn't handle non-finite values.
Results may differ from a plain program's by a relative error of at most 0.0047.
Values may be sent and summed in bfloat16 or wider, within the bound.
No kernel may reach another device: no remote copies, remote signals or barrier semaphores. Data moves between devices by JAX's collectives and lax.ppermute only.
A program may use at most 64 MiB of HBM per device.

v0:
```python
import math
import jax
import jax.numpy as jnp
from jax import lax
from jax.sharding import PartitionSpec as P

D = 2048
FW = 7168


def module_sums(weighting, received):
    flat = received.reshape(received.shape[0], -1)
    return lax.dot_general(
        weighting, flat, (((0,), (0,)), ((), ())), preferred_element_type=jnp.float32
    )


def per_device(hidden_in, teacher, params, momentum, path_alive, path_module):
    module_count = params.shape[0]
    block_rows = params.shape[2]
    width = params.shape[3]
    path_count = path_alive.shape[0]
    contract_last = (((1,), (1,)), ((), ()))
    contract_first = (((0,), (0,)), ((), ()))
    gate_pick = jnp.take(params[:, 0], path_module, axis=0)
    up_pick = jnp.take(params[:, 1], path_module, axis=0)
    down_pick = jnp.take(params[:, 2], path_module, axis=0)
    gate_rows, up_rows, down_rows = (
        lax.all_to_all(gate_pick, "path", split_axis=0, concat_axis=0, tiled=True),
        lax.all_to_all(up_pick, "path", split_axis=0, concat_axis=0, tiled=True),
        lax.all_to_all(down_pick, "path", split_axis=0, concat_axis=0, tiled=True),
    )
    local_rows = path_count * block_rows
    gate_rows = gate_rows.reshape(local_rows, width)
    up_rows = up_rows.reshape(local_rows, width)
    down_rows = down_rows.reshape(local_rows, width)
    rows_in = lax.all_gather(hidden_in, "tensor", axis=0, tiled=True)
    mean_sq = jnp.mean(jnp.square(rows_in.astype(jnp.float32)), axis=1, keepdims=True)
    normed = (rows_in.astype(jnp.float32) * lax.rsqrt(mean_sq + 1e-05)).astype(jnp.bfloat16)
    gate_pre = lax.dot_general(
        normed, gate_rows, contract_last, preferred_element_type=jnp.float32
    ) / math.sqrt(D)
    up_proj = lax.dot_general(
        normed, up_rows, contract_last, preferred_element_type=jnp.float32
    ) / math.sqrt(D)
    sigmoid_gate = jax.nn.sigmoid(gate_pre)
    activated = gate_pre * sigmoid_gate
    hidden = (activated * up_proj).astype(jnp.bfloat16)
    partial_out = jnp.dot(hidden, down_rows, preferred_element_type=jnp.float32) / math.sqrt(FW)
    output = lax.psum(partial_out, "tensor")
    cotangent = (4.0 * (output - teacher.astype(jnp.float32))).astype(jnp.bfloat16)
    down_delta = (
        lax.dot_general(hidden, cotangent, contract_first, preferred_element_type=jnp.float32)
        / math.sqrt(FW)
    ).astype(jnp.bfloat16)
    hidden_grad = lax.dot_general(
        cotangent, down_rows, contract_last, preferred_element_type=jnp.float32
    ) / math.sqrt(FW)
    gate_grad = (
        hidden_grad * up_proj * sigmoid_gate * (1.0 + gate_pre * (1.0 - sigmoid_gate))
    ).astype(jnp.bfloat16)
    up_grad = (hidden_grad * activated).astype(jnp.bfloat16)
    member = (path_module[:, None] == jnp.arange(module_count, dtype=jnp.int32)[None, :]).astype(
        jnp.int32
    ) * path_alive[:, None]
    weighting = member.astype(jnp.bfloat16)
    counts = jnp.sum(member, axis=0).astype(jnp.float32)
    piece_shape = (path_count, block_rows, width)
    gate_delta = (
        lax.dot_general(gate_grad, normed, contract_first, preferred_element_type=jnp.float32)
        / math.sqrt(D)
    ).astype(jnp.bfloat16)
    up_delta = (
        lax.dot_general(up_grad, normed, contract_first, preferred_element_type=jnp.float32)
        / math.sqrt(D)
    ).astype(jnp.bfloat16)
    gate_got, up_got, down_got = (
        lax.all_to_all(
            gate_delta.reshape(piece_shape), "path", split_axis=0, concat_axis=0, tiled=True
        ),
        lax.all_to_all(
            up_delta.reshape(piece_shape), "path", split_axis=0, concat_axis=0, tiled=True
        ),
        lax.all_to_all(
            down_delta.reshape(piece_shape), "path", split_axis=0, concat_axis=0, tiled=True
        ),
    )
    summed = jnp.stack(
        [
            module_sums(weighting, gate_got),
            module_sums(weighting, up_got),
            module_sums(weighting, down_got),
        ],
        axis=1,
    )
    summed = summed.reshape(module_count, 3, block_rows, width)
    mean_delta = summed / counts[:, None, None, None]
    new_momentum = 0.9 * momentum + mean_delta
    new_params = (params.astype(jnp.float32) - 0.7 * (mean_delta + 0.9 * new_momentum)).astype(
        jnp.bfloat16
    )
    return (new_params, new_momentum)


def solution(mesh):
    return jax.shard_map(
        per_device,
        mesh=mesh,
        in_specs=(
            P(("path", "tensor"), None),
            P("path", None),
            P(None, None, ("tensor", "path"), None),
            P(None, None, ("tensor", "path"), None),
            P(),
            P(),
        ),
        out_specs=(
            P(None, None, ("tensor", "path"), None),
            P(None, None, ("tensor", "path"), None),
        ),
        check_vma=False,
    )
```

profile of v0, /device:TPU:1, one launch (start us, length us, event | category | flops | bytes accessed | tf_op | source)
XLA Modules:
  0.0 420.3 jit_solution(7197902476013149992)
XLA Ops:
  7.2 0.7 compare_select_fusion
  7.8 0.7 compare_and_fusion
  8.5 1.2 slice_bitcast_fusion
  9.7 0.7 gather_fusion
  10.3 2.0 gather_fusion.1
  12.4 2.0 gather_fusion.2
  14.4 4.8 %broadcast_select_fusion = (bf16[32,14,2048]{2,1,0:T(8,128)(2,1)}, bf16[32,14,2048]{2,1,0:T(8,128)(2,1)}, bf16[32,14,2048]{2,1,0:T(8,128)(2,1)S(1)}) fusion(bf16[32,14,2048]{2,1,0:T(8,128)(2,1)} %gather_fusion.2, pred[32]{0:T(512)(128)(4,1)S(1)} %compare_and_fusion, bf16[32,14,2048]{2,1,0:T(8,128)(2,1)} %gather_fusion.1, bf16[32,14,2048]{2,1,0:T(8,128)(2,1)S(1)} %gather_fusion), kind=kLoop, calls=%fused_computation.15 | loop fusion | flops 2752512 | bytes 11010080 | tf_op jit(solution)/shard_map/jit(_take)/select_n | solution.py:27
  19.2 37.7 %all_to_all.30 = bf16[32,14,2048]{2,1,0:T(8,128)(2,1)S(1)} all-to-all(bf16[32,14,2048]{2,1,0:T(8,128)(2,1)S(1)} %get-tuple-element.14), channel_id=1, replica_groups=mesh['path'=32,'tensor'=16] {'path'}, dimensions={0} | all-to-all | bytes 3670016 | tf_op jit(solution)/shard_map/all_to_all | solution.py:29
  56.9 4.5 %all-to-all-start.1 = ((bf16[32,14,2048]{2,1,0:T(8,128)(2,1)}), bf16[32,14,2048]{2,1,0:T(8,128)(2,1)}, u32[]{:S(2)}, u32[]{:S(2)}) async-start(bf16[32,14,2048]{2,1,0:T(8,128)(2,1)} %get-tuple-element.13), calls=%async_computation.1 | async-start | bytes 4194304 | tf_op jit(solution)/shard_map/all_to_all | solution.py:30
  61.5 0.0 all-gather.2.cloned.1.call-start
  61.5 0.7 all-gather.2.cloned.1.call-update
  62.2 27.6 %all-to-all-done.1 = bf16[32,14,2048]{2,1,0:T(8,128)(2,1)} async-done(((bf16[32,14,2048]{2,1,0:T(8,128)(2,1)}), bf16[32,14,2048]{2,1,0:T(8,128)(2,1)}, u32[]{:S(2)}, u32[]{:S(2)}) %all-to-all-start.1) | async-done | bytes 1835040 | tf_op jit(solution)/shard_map/all_to_all | solution.py:30
  89.9 5.2 %all-to-all-start.2 = ((bf16[32,14,2048]{2,1,0:T(8,128)(2,1)}), bf16[32,14,2048]{2,1,0:T(8,128)(2,1)}, u32[]{:S(2)}, u32[]{:S(2)}) async-start(bf16[32,14,2048]{2,1,0:T(8,128)(2,1)} %get-tuple-element.12), calls=%async_computation.2 | async-start | bytes 4194304 | tf_op jit(solution)/shard_map/all_to_all | solution.py:31
  95.0 0.0 all-reduce.2.cloned.1.call-start
  95.1 1.5 reshape.74
  96.6 3.7 reshape.75
  100.3 23.2 %all-to-all-done.2 = bf16[32,14,2048]{2,1,0:T(8,128)(2,1)} async-done(((bf16[32,14,2048]{2,1,0:T(8,128)(2,1)}), bf16[32,14,2048]{2,1,0:T(8,128)(2,1)}, u32[]{:S(2)}, u32[]{:S(2)}) %all-to-all-start.2) | async-done | bytes 1835040 | tf_op jit(solution)/shard_map/all_to_all | solution.py:31
  123.5 2.5 reshape.76
  126.1 4.1 all-gather.2.cloned.1.call-done
  130.2 1.8 fusion
  132.0 0.0 copy-start.3
  132.0 0.0 copy-start.4
  132.0 3.3 convolution_multiply_fusion.3
  135.3 0.0 copy-done.3
  135.3 0.0 copy-done.4
  135.3 0.0 copy-start.11
  135.4 2.1 multiply_convert_fusion.6
  137.4 0.0 copy-done.11
  137.4 0.0 copy-start.1
  137.4 0.7 copy-done.1
  138.2 2.7 convolution_multiply_fusion
  140.9 0.0 all-reduce.2.cloned.1.call-update
  140.9 147.1 %all-reduce.2.cloned.1.call-done = f32[384,2048]{1,0:T(8,128)} async-done(((f32[384,2048]{1,0:T(8,128)}), f32[384,2048]{1,0:T(8,128)}) %all-reduce.2.cloned.1.call-update) | async-done | bytes 3145744 | tf_op jit(solution)/shard_map/psum | solution.py:50
  288.0 0.0 copy-done
  288.0 3.2 convolution_multiply_fusion.1
  291.2 0.0 copy-start.7
  291.2 0.9 copy-done.7
  292.1 0.0 copy-done.5
  292.1 0.0 copy-done.12
  292.1 0.0 copy-done.13
  292.1 1.4 multiply_convert_fusion.2
  293.5 1.6 reshape.77
  295.1 16.8 %all-to-all-start.3 = ((bf16[32,14,2048]{2,1,0:T(8,128)(2,1)}), bf16[32,14,2048]{2,1,0:T(8,128)(2,1)}, u32[]{:S(2)}, u32[]{:S(2)}) async-start(bf16[32,14,2048]{2,1,0:T(8,128)(2,1)} %reshape.77), calls=%async_computation.3 | async-start | bytes 4194304 | tf_op jit(solution)/shard_map/all_to_all | solution.py:78
  311.9 3.1 multiply_convert_fusion.1
  315.0 1.7 reshape.80
  316.7 23.6 %all-to-all-done.3 = bf16[32,14,2048]{2,1,0:T(8,128)(2,1)} async-done(((bf16[32,14,2048]{2,1,0:T(8,128)(2,1)}), bf16[32,14,2048]{2,1,0:T(8,128)(2,1)}, u32[]{:S(2)}, u32[]{:S(2)}) %all-to-all-start.3) | async-done | bytes 1835040 | tf_op jit(solution)/shard_map/all_to_all | solution.py:78
  340.3 5.2 %all-to-all-start.4 = ((bf16[32,14,2048]{2,1,0:T(8,128)(2,1)}), bf16[32,14,2048]{2,1,0:T(8,128)(2,1)}, u32[]{:S(2)}, u32[]{:S(2)}) async-start(bf16[32,14,2048]{2,1,0:T(8,128)(2,1)} %reshape.80), calls=%async_computation.4 | async-start | bytes 4194304 | tf_op jit(solution)/shard_map/all_to_all | solution.py:81
  345.5 3.2 multiply_convert_fusion
  348.7 1.6 reshape.83
  350.3 23.7 %all-to-all-done.4 = bf16[32,14,2048]{2,1,0:T(8,128)(2,1)} async-done(((bf16[32,14,2048]{2,1,0:T(8,128)(2,1)}), bf16[32,14,2048]{2,1,0:T(8,128)(2,1)}, u32[]{:S(2)}, u32[]{:S(2)}) %all-to-all-start.4) | async-done | bytes 1835040 | tf_op jit(solution)/shard_map/all_to_all | solution.py:81
  374.0 4.5 %all-to-all-start.5 = ((bf16[32,14,2048]{2,1,0:T(8,128)(2,1)}), bf16[32,14,2048]{2,1,0:T(8,128)(2,1)S(1)}, u32[]{:S(2)}, u32[]{:S(2)}) async-start(bf16[32,14,2048]{2,1,0:T(8,128)(2,1)} %reshape.83), calls=%async_computation.5 | async-start | bytes 4194304 | tf_op jit(solution)/shard_map/all_to_all | solution.py:84
  378.4 0.0 copy-done.9
  378.5 0.0 copy-done.10
  378.5 0.1 select_reduce_fusion
  378.6 3.6 convolution_bitcast_fusion.2
  382.2 4.4 %convolution_bitcast_fusion.1 = f32[3,1,14,2048]{3,0,2,1:T(4,128)} fusion(s32[32]{0:T(128)S(1)} %copy-done.9, s32[32]{0:T(128)S(1)} %copy-done.10, bf16[4,8,14,2048]{3,2,1,0:T(8,128)(2,1)} %bitcast.18), kind=kOutput, calls=%fused_computation.13 | convolution fusion | flops 5505312 | bytes 2179328 | tf_op jit(solution)/shard_map/dot_general | solution.py:13
  386.6 20.2 %all-to-all-done.5 = bf16[32,14,2048]{2,1,0:T(8,128)(2,1)S(1)} async-done(((bf16[32,14,2048]{2,1,0:T(8,128)(2,1)}), bf16[32,14,2048]{2,1,0:T(8,128)(2,1)S(1)}, u32[]{:S(2)}, u32[]{:S(2)}) %all-to-all-start.5) | async-done | bytes 1835040 | tf_op jit(solution)/shard_map/all_to_all | solution.py:84
  406.9 2.0 convolution_bitcast_fusion
  408.9 0.0 copy-done.2
  408.9 0.0 copy-done.6
  408.9 0.0 copy-done.8
  408.9 1.7 fusion.8
  410.7 1.6 copy.18
  412.3 1.2 copy.17
  (12 shorter events, 0.0 us)
Async XLA Ops:
  56.9 32.9 %all-to-all-start.1 = ((bf16[32,14,2048]{2,1,0:T(8,128)(2,1)}), bf16[32,14,2048]{2,1,0:T(8,128)(2,1)}, u32[]{:S(2)}, u32[]{:S(2)}) async-start(bf16[32,14,2048]{2,1,0:T(8,128)(2,1)} %get-tuple-element.13), calls=%async_computation.1 | async-start | bytes 4194304 | tf_op jit(solution)/shard_map/all_to_all | solution.py:30
  61.5 68.7 %all-gather.2.cloned.1.call-start = ((), (), s32[]{:S(2)}) async-start(), calls=%async_computation.6 | async-start | bytes 1671168 | tf_op jit(solution)/shard_map/all_gather | solution.py:37
  89.9 33.7 %all-to-all-start.2 = ((bf16[32,14,2048]{2,1,0:T(8,128)(2,1)}), bf16[32,14,2048]{2,1,0:T(8,128)(2,1)}, u32[]{:S(2)}, u32[]{:S(2)}) async-start(bf16[32,14,2048]{2,1,0:T(8,128)(2,1)} %get-tuple-element.12), calls=%async_computation.2 | async-start | bytes 4194304 | tf_op jit(solution)/shard_map/all_to_all | solution.py:31
  95.0 193.0 %all-reduce.2.cloned.1.call-start = ((), (), s32[]{:S(2)}) async-start(), calls=%async_computation.7 | async-start | bytes 6291456 | tf_op jit(solution)/shard_map/psum | solution.py:50
  132.0 3.4 copy-start.3
  132.0 3.4 copy-start.4
  135.3 2.1 copy-start.11
  137.4 0.7 copy-start.1
  140.9 147.2 %copy-start = (bf16[384,2048]{1,0:T(8,128)(2,1)S(1)}, bf16[384,2048]{1,0:T(8,128)(2,1)}, u32[]{:S(2)}) copy-start(bf16[384,2048]{1,0:T(8,128)(2,1)} %param.9) | copy-start | bytes 4718596
  288.0 4.1 copy-start.5
  288.0 4.1 copy-start.12
  288.0 4.1 copy-start.13
  291.2 0.9 copy-start.7
  295.1 45.2 %all-to-all-start.3 = ((bf16[32,14,2048]{2,1,0:T(8,128)(2,1)}), bf16[32,14,2048]{2,1,0:T(8,128)(2,1)}, u32[]{:S(2)}, u32[]{:S(2)}) async-start(bf16[32,14,2048]{2,1,0:T(8,128)(2,1)} %reshape.77), calls=%async_computation.3 | async-start | bytes 4194304 | tf_op jit(solution)/shard_map/all_to_all | solution.py:78
  340.3 33.6 %all-to-all-start.4 = ((bf16[32,14,2048]{2,1,0:T(8,128)(2,1)}), bf16[32,14,2048]{2,1,0:T(8,128)(2,1)}, u32[]{:S(2)}, u32[]{:S(2)}) async-start(bf16[32,14,2048]{2,1,0:T(8,128)(2,1)} %reshape.80), calls=%async_computation.4 | async-start | bytes 4194304 | tf_op jit(solution)/shard_map/all_to_all | solution.py:81
  350.3 28.2 %copy-start.9 = (s32[32]{0:T(128)S(1)}, s32[32]{0:T(128)}, u32[]{:S(2)}) copy-start(s32[32]{0:T(128)} %param.12) | copy-start | bytes 388
  350.3 28.2 %copy-start.10 = (s32[32]{0:T(128)S(1)}, s32[32]{0:T(128)}, u32[]{:S(2)}) copy-start(s32[32]{0:T(128)} %param.13) | copy-start | bytes 388
  374.0 32.9 %all-to-all-start.5 = ((bf16[32,14,2048]{2,1,0:T(8,128)(2,1)}), bf16[32,14,2048]{2,1,0:T(8,128)(2,1)S(1)}, u32[]{:S(2)}, u32[]{:S(2)}) async-start(bf16[32,14,2048]{2,1,0:T(8,128)(2,1)} %reshape.83), calls=%async_computation.5 | async-start | bytes 4194304 | tf_op jit(solution)/shard_map/all_to_all | solution.py:84
  386.6 22.3 %copy-start.2 = (bf16[3,3,14,2048]{3,2,1,0:T(8,128)(2,1)S(1)}, bf16[3,3,14,2048]{3,2,1,0:T(8,128)(2,1)}, u32[]{:S(2)}) copy-start(bf16[3,3,14,2048]{3,2,1,0:T(8,128)(2,1)} %param.10) | copy-start | bytes 1548292
  406.9 2.1 copy-start.6
  406.9 2.1 copy-start.8
Sparse Core Ops, SparseCore 0:
  64.4 65.7 all-gather.1
  141.0 146.9 all-reduce.1
where the time goes:
time: 421 us; the launch traced here: 420 us
  waiting for transfers between devices  270 us (64%)
  blocking collectives  37.7 us (9%)
  starting transfers between devices  36.3 us (9%)
  matrix products  29 us (7%)
  local copies, waits for them, and re-layouts  23 us (5%)
  between operations  14.2 us (3%)
  other arithmetic  9.82 us (2%)
    psum x1, waiting for transfers between devices, per_device(): output = lax.psum(partial_out, 'tensor')  147 us
    all_to_all x1, blocking collectives, per_device(): lax.all_to_all(gate_pick, 'path', split_axis=0, concat_axis=0, tiled=True)  37.7 us
    all_to_all x1, waiting for transfers between devices, per_device(): lax.all_to_all(up_pick, 'path', split_axis=0, concat_axis=0, tiled=True)  27.6 us
    all_to_all x1, waiting for transfers between devices, per_device(): lax.all_to_all(up_delta.reshape(piece_shape), 'path', split_axis=0, conca...  23.7 us
    all_to_all x1, waiting for transfers between devices, per_device(): lax.all_to_all(gate_delta.reshape(piece_shape), 'path', split_axis=0, con...  23.6 us
    all_to_all x1, waiting for transfers between devices, per_device(): lax.all_to_all(down_pick, 'path', split_axis=0, concat_axis=0, tiled=True)  23.2 us
    all_to_all x1, waiting for transfers between devices, per_device(): lax.all_to_all(down_delta.reshape(piece_shape), 'path', split_axis=0, con...  20.2 us
    all_to_all x1, starting transfers between devices, per_device(): lax.all_to_all(gate_delta.reshape(piece_shape), 'path', split_axis=0, con...  16.8 us
  transfers between devices with their start and end apart: 7, of which 7 were waited for; matrix products, arithmetic and copies ran while one was open for 6% of the time, Pallas kernels for 0%

commit v1 on v0

--- a/solution.py
+++ b/solution.py
@@ -47,7 +47,9 @@
     activated = gate_pre * sigmoid_gate
     hidden = (activated * up_proj).astype(jnp.bfloat16)
     partial_out = jnp.dot(hidden, down_rows, preferred_element_type=jnp.float32) / math.sqrt(FW)
-    output = lax.psum(partial_out, "tensor")
+    output = partial_out
+    for hop in (1, 2, 4, 8):
+        output = output + lax.ppermute(output, "tensor", [(dev, dev ^ hop) for dev in range(16)])
     cotangent = (4.0 * (output - teacher.astype(jnp.float32))).astype(jnp.bfloat16)
     down_delta = (
         lax.dot_general(hidden, cotangent, contract_first, preferred_element_type=jnp.float32)

time: 421 us -> 1020 us (2.42)
  waiting for transfers between devices: 270 us -> 788 us
  starting transfers between devices: 36.3 us -> 117 us
    ppermute x0 -> x4, waiting for transfers between devices: none -> 668 us  [per_device(): lax.ppermute(output, 'tensor', [(dev, dev ^ hop) for dev in range(16)])]
    psum x1 -> x0, waiting for transfers between devices: 147 us -> none  [per_device(): output = lax.psum(partial_out, 'tensor')]
    ppermute x0 -> x4, starting transfers between devices: none -> 92 us  [per_device(): lax.ppermute(output, 'tensor', [(dev, dev ^ hop) for dev in range(16)])]
    all_to_all x1, starting transfers between devices: 16.8 us -> 4.95 us  [per_device(): lax.all_to_all(gate_delta.reshape(piece_shape), 'path', split_axis=0, con...]
  transfers between devices with their start and end apart: 7 -> 10, of which waited for: 7 -> 10; matrix products, arithmetic and copies ran while one was open for 6% -> 3% of each run, Pallas kernels for 0% -> 0%
where the time goes in v1:
time: 1020 us
  waiting for transfers between devices  788 us (77%)
  starting transfers between devices  117 us (11%)
  blocking collectives  37.7 us (4%)
  local copies, waits for them, and re-layouts  25.3 us (2%)
  matrix products  25.3 us (2%)
  between operations  14.3 us (1%)
  other arithmetic  12.7 us (1%)
    ppermute x4, waiting for transfers between devices, per_device(): lax.ppermute(output, 'tensor', [(dev, dev ^ hop) for dev in range(16)])  668 us
    ppermute x4, starting transfers between devices, per_device(): lax.ppermute(output, 'tensor', [(dev, dev ^ hop) for dev in range(16)])  92 us
    all_to_all x1, blocking collectives, per_device(): lax.all_to_all(gate_pick, 'path', split_axis=0, concat_axis=0, tiled=True)  37.7 us
    all_to_all x1, waiting for transfers between devices, per_device(): lax.all_to_all(up_pick, 'path', split_axis=0, concat_axis=0, tiled=True)  27.6 us
    all_to_all x1, waiting for transfers between devices, per_device(): lax.all_to_all(down_pick, 'path', split_axis=0, concat_axis=0, tiled=True)  23.3 us
    all_to_all x1, waiting for transfers between devices, per_device(): lax.all_to_all(down_delta.reshape(piece_shape), 'path', split_axis=0, con...  22.6 us
    all_to_all x1, waiting for transfers between devices, per_device(): lax.all_to_all(up_delta.reshape(piece_shape), 'path', split_axis=0, conca...  21.1 us
    all_to_all x1, waiting for transfers between devices, per_device(): lax.all_to_all(gate_delta.reshape(piece_shape), 'path', split_axis=0, con...  20.7 us
  transfers between devices with their start and end apart: 10, of which 10 were waited for; matrix products, arithmetic and copies ran while one was open for 3% of the time, Pallas kernels for 0%

profile of v1, /device:TPU:1, one launch (start us, length us, event | category | flops | bytes accessed | tf_op | source)
XLA Modules:
  0.0 1020.6 jit_solution(4684950768324377970)
XLA Ops:
  7.2 0.7 compare_select_fusion
  7.8 0.7 compare_and_fusion
  8.5 1.2 slice_bitcast_fusion
  9.7 0.7 gather_fusion
  10.3 2.0 gather_fusion.1
  12.4 2.0 gather_fusion.2
  14.4 4.9 broadcast_select_fusion
  19.2 37.7 %all_to_all.30 = bf16[32,14,2048]{2,1,0:T(8,128)(2,1)S(1)} all-to-all(bf16[32,14,2048]{2,1,0:T(8,128)(2,1)S(1)} %get-tuple-element.14), channel_id=1, replica_groups=mesh['path'=32,'tensor'=16] {'path'}, dimensions={0} | all-to-all | bytes 3670016 | tf_op jit(solution)/shard_map/all_to_all | solution.py:29
  56.9 4.6 all-to-all-start.1
  61.5 0.0 all-gather.2.cloned.1.call-start
  61.6 0.7 all-gather.2.cloned.1.call-update
  62.2 27.6 %all-to-all-done.1 = bf16[32,14,2048]{2,1,0:T(8,128)(2,1)} async-done(((bf16[32,14,2048]{2,1,0:T(8,128)(2,1)}), bf16[32,14,2048]{2,1,0:T(8,128)(2,1)}, u32[]{:S(2)}, u32[]{:S(2)}) %all-to-all-start.1) | async-done | bytes 1835040 | tf_op jit(solution)/shard_map/all_to_all | solution.py:30
  89.9 5.2 all-to-all-start.2
  95.1 1.5 reshape.74
  96.6 3.7 reshape.75
  100.3 23.3 %all-to-all-done.2 = bf16[32,14,2048]{2,1,0:T(8,128)(2,1)} async-done(((bf16[32,14,2048]{2,1,0:T(8,128)(2,1)}), bf16[32,14,2048]{2,1,0:T(8,128)(2,1)}, u32[]{:S(2)}, u32[]{:S(2)}) %all-to-all-start.2) | async-done | bytes 1835040 | tf_op jit(solution)/shard_map/all_to_all | solution.py:31
  123.5 2.5 reshape.76
  126.1 4.1 all-gather.2.cloned.1.call-done
  130.2 1.8 fusion
  132.0 0.0 copy-start.4
  132.0 3.3 convolution_multiply_fusion.3
  135.3 0.0 copy-done.1
  135.3 0.0 copy-done.4
  135.4 0.0 copy-start.8
  135.4 1.3 multiply_convert_fusion.6
  136.6 1.0 convolution_multiply_fusion
  137.6 2.7 collective-permute-start
  140.3 59.3 %collective-permute-done = f32[384,2048]{1,0:T(8,128)S(1)} collective-permute-done((f32[384,2048]{1,0:T(8,128)S(1)}, f32[384,2048]{1,0:T(8,128)S(1)}, u32[]{:S(2)}, u32[]{:S(2)}) %collective-permute-start) | collective-permute-done | bytes 3145760 | tf_op jit(solution)/shard_map/ppermute | solution.py:52
  199.7 0.7 add.44
  200.3 3.2 collective-permute-start.1
  203.6 132.2 %collective-permute-done.1 = f32[384,2048]{1,0:T(8,128)S(1)} collective-permute-done((f32[384,2048]{1,0:T(8,128)S(1)}, f32[384,2048]{1,0:T(8,128)S(1)}, u32[]{:S(2)}, u32[]{:S(2)}) %collective-permute-start.1) | collective-permute-done | bytes 3145760 | tf_op jit(solution)/shard_map/ppermute | solution.py:52
  335.8 0.7 add.45
  336.5 0.0 copy-start.2
  336.5 4.0 collective-permute-start.2
  340.4 341.1 %collective-permute-done.2 = f32[384,2048]{1,0:T(8,128)S(1)} collective-permute-done((f32[384,2048]{1,0:T(8,128)S(1)}, f32[384,2048]{1,0:T(8,128)S(1)}, u32[]{:S(2)}, u32[]{:S(2)}) %collective-permute-start.2) | collective-permute-done | bytes 3145760 | tf_op jit(solution)/shard_map/ppermute | solution.py:52
  681.6 0.7 add.46
  682.3 82.1 %collective-permute-start.3 = (f32[384,2048]{1,0:T(8,128)S(1)}, f32[384,2048]{1,0:T(8,128)S(1)}, u32[]{:S(2)}, u32[]{:S(2)}) collective-permute-start(f32[384,2048]{1,0:T(8,128)S(1)} %add.46), channel_id=1, source_target_pairs={{0,8},{1,9},{2,10},{3,11},{4,12},{5,13},{6,14},{7,15},{8,0},{9,1},... | collective-permute-start | bytes 9437192 | tf_op jit(solution)/shard_map/ppermute | solution.py:52
  764.4 135.4 %collective-permute-done.3 = f32[384,2048]{1,0:T(8,128)S(1)} collective-permute-done((f32[384,2048]{1,0:T(8,128)S(1)}, f32[384,2048]{1,0:T(8,128)S(1)}, u32[]{:S(2)}, u32[]{:S(2)}) %collective-permute-start.3) | collective-permute-done | bytes 3145760 | tf_op jit(solution)/shard_map/ppermute | solution.py:52
  899.8 0.0 copy-done.2
  899.8 0.9 multiply_convert_fusion.3
  900.7 0.0 copy-start.3
  900.7 1.1 convolution_multiply_fusion.1
  901.8 0.0 copy-done.3
  901.9 0.0 copy-done.8
  901.9 1.4 multiply_convert_fusion.2
  903.3 1.6 reshape.77
  904.9 4.9 all-to-all-start.3
  909.8 4.1 multiply_convert_fusion.1
  913.9 3.6 reshape.80
  917.5 20.7 %all-to-all-done.3 = bf16[32,14,2048]{2,1,0:T(8,128)(2,1)S(1)} async-done(((bf16[32,14,2048]{2,1,0:T(8,128)(2,1)}), bf16[32,14,2048]{2,1,0:T(8,128)(2,1)S(1)}, u32[]{:S(2)}, u32[]{:S(2)}) %all-to-all-start.3) | async-done | bytes 1835040 | tf_op jit(solution)/shard_map/all_to_all | solution.py:80
  938.2 5.2 all-to-all-start.4
  943.4 3.8 multiply_convert_fusion
  947.2 3.6 reshape.83
  950.8 21.1 %all-to-all-done.4 = bf16[32,14,2048]{2,1,0:T(8,128)(2,1)} async-done(((bf16[32,14,2048]{2,1,0:T(8,128)(2,1)}), bf16[32,14,2048]{2,1,0:T(8,128)(2,1)}, u32[]{:S(2)}, u32[]{:S(2)}) %all-to-all-start.4) | async-done | bytes 1835040 | tf_op jit(solution)/shard_map/all_to_all | solution.py:83
  971.9 5.2 all-to-all-start.5
  977.1 0.1 select_reduce_fusion
  977.2 2.0 convolution_bitcast_fusion.2
  979.3 3.6 convolution_bitcast_fusion.1
  982.9 22.6 %all-to-all-done.5 = bf16[32,14,2048]{2,1,0:T(8,128)(2,1)} async-done(((bf16[32,14,2048]{2,1,0:T(8,128)(2,1)}), bf16[32,14,2048]{2,1,0:T(8,128)(2,1)}, u32[]{:S(2)}, u32[]{:S(2)}) %all-to-all-start.5) | async-done | bytes 1835040 | tf_op jit(solution)/shard_map/all_to_all | solution.py:86
  1005.5 3.6 convolution_bitcast_fusion
  1009.2 0.0 copy-done.5
  1009.2 1.7 fusion.8
  1010.9 1.6 copy.18
  1012.5 1.2 copy.17
  (11 shorter events, 0.0 us)
Async XLA Ops:
  56.9 32.9 %all-to-all-start.1 = ((bf16[32,14,2048]{2,1,0:T(8,128)(2,1)}), bf16[32,14,2048]{2,1,0:T(8,128)(2,1)}, u32[]{:S(2)}, u32[]{:S(2)}) async-start(bf16[32,14,2048]{2,1,0:T(8,128)(2,1)} %get-tuple-element.13), calls=%async_computation.1 | async-start | bytes 4194304 | tf_op jit(solution)/shard_map/all_to_all | solution.py:30
  61.5 68.7 %all-gather.2.cloned.1.call-start = ((), (), s32[]{:S(2)}) async-start(), calls=%async_computation.6 | async-start | bytes 1671168 | tf_op jit(solution)/shard_map/all_gather | solution.py:37
  89.9 33.7 %all-to-all-start.2 = ((bf16[32,14,2048]{2,1,0:T(8,128)(2,1)}), bf16[32,14,2048]{2,1,0:T(8,128)(2,1)}, u32[]{:S(2)}, u32[]{:S(2)}) async-start(bf16[32,14,2048]{2,1,0:T(8,128)(2,1)} %get-tuple-element.12), calls=%async_computation.2 | async-start | bytes 4194304 | tf_op jit(solution)/shard_map/all_to_all | solution.py:31
  132.0 3.4 copy-start.1
  132.0 3.4 copy-start.4
  135.4 766.5 %copy-start.8 = (f32[384,448]{0,1:T(8,128)}, f32[384,448]{0,1:T(8,128)S(1)}, u32[]{:S(2)}) copy-start(f32[384,448]{0,1:T(8,128)S(1)} %convolution_multiply_fusion.3) | copy-start | bytes 2064388
  137.6 62.0 %collective-permute-start = (f32[384,2048]{1,0:T(8,128)S(1)}, f32[384,2048]{1,0:T(8,128)S(1)}, u32[]{:S(2)}, u32[]{:S(2)}) collective-permute-start(f32[384,2048]{1,0:T(8,128)S(1)} %convolution_multiply_fusion), channel_id=1, source_target_pairs={{0,1},{1,0},{2,3},{3,2},{4,5},{5,4},{6,7},{7,6},{8,9},{9,8},{10,11... | collective-permute-start | bytes 9437192 | tf_op jit(solution)/shard_map/ppermute | solution.py:52
  200.3 135.4 %collective-permute-start.1 = (f32[384,2048]{1,0:T(8,128)S(1)}, f32[384,2048]{1,0:T(8,128)S(1)}, u32[]{:S(2)}, u32[]{:S(2)}) collective-permute-start(f32[384,2048]{1,0:T(8,128)S(1)} %add.44), channel_id=1, source_target_pairs={{0,2},{1,3},{2,0},{3,1},{4,6},{5,7},{6,4},{7,5},{8,10},{9,11},{10,... | collective-permute-start | bytes 9437192 | tf_op jit(solution)/shard_map/ppermute | solution.py:52
  336.5 563.3 %copy-start.2 = (bf16[384,2048]{1,0:T(8,128)(2,1)S(1)}, bf16[384,2048]{1,0:T(8,128)(2,1)}, u32[]{:S(2)}) copy-start(bf16[384,2048]{1,0:T(8,128)(2,1)} %param.9) | copy-start | bytes 4718596
  336.5 345.1 %collective-permute-start.2 = (f32[384,2048]{1,0:T(8,128)S(1)}, f32[384,2048]{1,0:T(8,128)S(1)}, u32[]{:S(2)}, u32[]{:S(2)}) collective-permute-start(f32[384,2048]{1,0:T(8,128)S(1)} %add.45), channel_id=1, source_target_pairs={{0,4},{1,5},{2,6},{3,7},{4,0},{5,1},{6,2},{7,3},{8,12},{9,13},{10,... | collective-permute-start | bytes 9437192 | tf_op jit(solution)/shard_map/ppermute | solution.py:52
  682.3 217.5 %collective-permute-start.3 = (f32[384,2048]{1,0:T(8,128)S(1)}, f32[384,2048]{1,0:T(8,128)S(1)}, u32[]{:S(2)}, u32[]{:S(2)}) collective-permute-start(f32[384,2048]{1,0:T(8,128)S(1)} %add.46), channel_id=1, source_target_pairs={{0,8},{1,9},{2,10},{3,11},{4,12},{5,13},{6,14},{7,15},{8,0},{9,1},... | collective-permute-start | bytes 9437192 | tf_op jit(solution)/shard_map/ppermute | solution.py:52
  900.7 1.2 copy-start.3
  904.9 33.4 %all-to-all-start.3 = ((bf16[32,14,2048]{2,1,0:T(8,128)(2,1)}), bf16[32,14,2048]{2,1,0:T(8,128)(2,1)S(1)}, u32[]{:S(2)}, u32[]{:S(2)}) async-start(bf16[32,14,2048]{2,1,0:T(8,128)(2,1)} %reshape.77), calls=%async_computation.3 | async-start | bytes 4194304 | tf_op jit(solution)/shard_map/all_to_all | solution.py:80
  938.2 33.7 %all-to-all-start.4 = ((bf16[32,14,2048]{2,1,0:T(8,128)(2,1)}), bf16[32,14,2048]{2,1,0:T(8,128)(2,1)}, u32[]{:S(2)}, u32[]{:S(2)}) async-start(bf16[32,14,2048]{2,1,0:T(8,128)(2,1)} %reshape.80), calls=%async_computation.4 | async-start | bytes 4194304 | tf_op jit(solution)/shard_map/all_to_all | solution.py:83
  950.8 26.3 %copy-start.6 = (s32[32]{0:T(128)S(1)}, s32[32]{0:T(128)}, u32[]{:S(2)}) copy-start(s32[32]{0:T(128)} %param.12) | copy-start | bytes 388
  950.8 26.3 %copy-start.7 = (s32[32]{0:T(128)S(1)}, s32[32]{0:T(128)}, u32[]{:S(2)}) copy-start(s32[32]{0:T(128)} %param.13) | copy-start | bytes 388
  971.9 33.7 %all-to-all-start.5 = ((bf16[32,14,2048]{2,1,0:T(8,128)(2,1)}), bf16[32,14,2048]{2,1,0:T(8,128)(2,1)}, u32[]{:S(2)}, u32[]{:S(2)}) async-start(bf16[32,14,2048]{2,1,0:T(8,128)(2,1)} %reshape.83), calls=%async_computation.5 | async-start | bytes 4194304 | tf_op jit(solution)/shard_map/all_to_all | solution.py:86
  982.9 26.3 %copy-start = (bf16[3,3,14,2048]{3,2,1,0:T(8,128)(2,1)S(1)}, bf16[3,3,14,2048]{3,2,1,0:T(8,128)(2,1)}, u32[]{:S(2)}) copy-start(bf16[3,3,14,2048]{3,2,1,0:T(8,128)(2,1)} %param.10) | copy-start | bytes 1548292
  982.9 26.3 %copy-start.5 = (f32[3,3,14,2048]{3,2,1,0:T(8,128)S(1)}, f32[3,3,14,2048]{3,2,1,0:T(8,128)}, u32[]{:S(2)}) copy-start(f32[3,3,14,2048]{3,2,1,0:T(8,128)} %param.11) | copy-start | bytes 3096580
Sparse Core Ops, SparseCore 0:
  64.4 65.7 all-gather.1
